TPU v7x, 256 devices: a whole 4x4x8 slice. The times are simulated.
256 devices in a mesh: seq: 16 (over y, x), chan: 16 (over z, core).
Axes of the slice: x: 4, y: 4, z: 8, core: 2. Of those that a mesh axis runs over, the one named last changes fastest.
Arguments:
- layer_input: bfloat16 [2048, 8192], P('seq', 'chan'), may hold values from -6 to 6
- value_pre: bfloat16 [2048, 8192], P('seq', 'chan'), may hold values from -6 to 6
- gate_act: bfloat16 [2048, 8192], P('seq', 'chan'), may hold values from -6 to 6
- key_act: bfloat16 [2048, 8192], P('seq', 'chan'), may hold values from -6 to 6
- short_taps: float32 [3, 8192], P(None, 'chan'), may hold values from -3 to 3
- long_filter: float32 [2048, 8192], P('seq', 'chan'), may hold values from -0.125 to 0.125
- grad_out: bfloat16 [2048, 8192], P('seq', 'chan'), may hold values from -6 to 6
Outputs:
- grad_gate: bfloat16 [2048, 8192], P('seq', 'chan')
- grad_key: bfloat16 [2048, 8192], P('seq', 'chan')
- grad_value: bfloat16 [2048, 8192], P('seq', 'chan')
- grad_taps: float32 [3, 8192], P(None, 'chan')
- grad_filter: float32 [2048, 8192], P('seq', 'chan')
- grad_proj: float32 [8192, 8192], P('chan', 'seq')
All inputs are finite; a program needn't handle non-finite values.
Results may differ from a plain program's by a relative error of at most 0.0029.
Values may be sent and summed in bfloat16 or wider, within the bound.
No kernel may reach another device: no remote copies, remote signals or barrier semaphores. Data moves between devices by JAX's collectives and lax.ppermute only.
A program may use at most 128 MiB of HBM per device.

v0:
```python
import numpy as np

import jax
import jax.numpy as jnp
from jax import lax
from jax.sharding import PartitionSpec as P

F32 = jnp.float32
BF16 = jnp.bfloat16
PRECISE = lax.Precision.HIGHEST


def angles(rows, cols, period):
    product = np.outer(np.arange(rows), np.arange(cols)) % period
    return product.astype(np.float64) * (2.0 * np.pi / period)


def dft_tables(blocks, width):
    freq_blocks = 2 * blocks
    total = freq_blocks * width
    outer = angles(freq_blocks, blocks, freq_blocks)
    stage_a = np.concatenate([np.cos(outer), -np.sin(outer)], axis=0)
    twist = angles(freq_blocks, width, total)
    twist_cos = np.cos(twist)[:, None, None, :]
    twist_sin = np.sin(twist)[:, None, None, :]
    inner = angles(width, width, width)
    inner_cos, inner_sin = np.cos(inner), np.sin(inner)
    stage_b = np.concatenate(
        [np.concatenate([inner_cos, -inner_sin], axis=1), np.concatenate([inner_sin, inner_cos], axis=1)],
        axis=0,
    )
    back_b = np.concatenate(
        [np.concatenate([inner_cos, inner_sin], axis=1), np.concatenate([-inner_sin, inner_cos], axis=1)],
        axis=0,
    )
    back_a = np.concatenate([np.cos(outer).T, -np.sin(outer).T], axis=1) / total
    as_f32 = lambda a: jnp.asarray(a.astype(np.float32))
    return tuple(as_f32(a) for a in (stage_a, twist_cos, twist_sin, stage_b, back_b, back_a))


def long_mix(stacked):
    blocks, _, _, width = stacked.shape
    stage_a, twist_cos, twist_sin, stage_b, back_b, back_a = dft_tables(blocks, width)
    freq_blocks = 2 * blocks
    outer = jnp.einsum("kp,pscm->kscm", stage_a, stacked, precision=PRECISE)
    outer_re, outer_im = outer[:freq_blocks], outer[freq_blocks:]
    turned_re = outer_re * twist_cos + outer_im * twist_sin
    turned_im = outer_im * twist_cos - outer_re * twist_sin
    spec = jnp.einsum("kscm,mn->kscn", turned_re, stage_b[:width], precision=PRECISE) + jnp.einsum(
        "kscm,mn->kscn", turned_im, stage_b[width:], precision=PRECISE
    )
    spec_re, spec_im = spec[..., :width], spec[..., width:]
    filt_re, sig_re, grad_re = spec_re[:, 0], spec_re[:, 1], spec_re[:, 2]
    filt_im, sig_im, grad_im = spec_im[:, 0], spec_im[:, 1], spec_im[:, 2]
    prod_re = jnp.stack(
        [
            filt_re * sig_re - filt_im * sig_im,
            filt_re * grad_re + filt_im * grad_im,
            sig_re * grad_re + sig_im * grad_im,
        ],
        axis=1,
    )
    prod_im = jnp.stack(
        [
            filt_re * sig_im + filt_im * sig_re,
            filt_re * grad_im - filt_im * grad_re,
            sig_re * grad_im - sig_im * grad_re,
        ],
        axis=1,
    )
    inner = jnp.einsum("kscn,nm->kscm", prod_re, back_b[:width], precision=PRECISE) + jnp.einsum(
        "kscn,nm->kscm", prod_im, back_b[width:], precision=PRECISE
    )
    inner_re, inner_im = inner[..., :width], inner[..., width:]
    back_re = inner_re * twist_cos - inner_im * twist_sin
    back_im = inner_re * twist_sin + inner_im * twist_cos
    both = jnp.concatenate([back_re, back_im], axis=0)
    return jnp.einsum("pk,kscm->pscm", back_a, both, precision=PRECISE)


def shift_back(x, by, lane):
    earlier = jnp.concatenate([jnp.zeros_like(x[:1]), x[:-1]], axis=0)
    return jnp.where(lane < by, jnp.roll(earlier, by, axis=-1), jnp.roll(x, by, axis=-1))


def shift_ahead(x, by, lane):
    later = jnp.concatenate([x[1:], jnp.zeros_like(x[:1])], axis=0)
    width = x.shape[-1]
    return jnp.where(lane >= width - by, jnp.roll(later, -by, axis=-1), jnp.roll(x, -by, axis=-1))


def to_tokens_in_lanes(block, parts):
    rows, cols = block.shape[-2:]
    swapped = jnp.swapaxes(block, -1, -2)
    return swapped.reshape(block.shape[:-2] + (parts, cols // parts, rows))


def from_tokens_in_lanes(block):
    lead = block.shape[:-3]
    parts, sub, rows = block.shape[-3:]
    return jnp.swapaxes(block.reshape(lead + (parts * sub, rows)), -1, -2)


def on_device(layer_input, value_pre, gate_act, key_act, short_taps, long_filter, grad_out):
    n_seq = lax.axis_size("seq")
    n_chan = lax.axis_size("chan")
    me = lax.axis_index("seq")
    tap_count = short_taps.shape[0]
    sub = value_pre.shape[1] // n_seq

    inputs_all = lax.all_gather(layer_input, "seq", axis=0, tiled=True)

    halves = to_tokens_in_lanes(jnp.stack([value_pre, gate_act, key_act, grad_out]), n_seq)
    halves = lax.all_to_all(halves, "seq", split_axis=1, concat_axis=1, tiled=True)
    filt = lax.all_to_all(to_tokens_in_lanes(long_filter, n_seq), "seq", split_axis=0, concat_axis=0, tiled=True)
    value_t = halves[0].astype(F32)
    gate_t = halves[1].astype(F32)
    key_t = halves[2].astype(F32)
    gout_t = halves[3].astype(F32)
    taps = lax.dynamic_slice_in_dim(short_taps, me * sub, sub, axis=1)[:, :, None]
    lane = lax.broadcasted_iota(jnp.int32, value_t.shape, 2)

    value_shifted = [value_t] + [shift_back(value_t, j, lane) for j in range(1, tap_count)]
    conv_val = taps[0] * value_shifted[0]
    for tap_index in range(1, tap_count):
        conv_val = conv_val + taps[tap_index] * value_shifted[tap_index]
    signal = key_t * conv_val
    grad_mix = gout_t * gate_t
    mixed = long_mix(jnp.stack([filt, signal, grad_mix], axis=1))
    mix_out, grad_signal, grad_filter = mixed[:, 0], mixed[:, 1], mixed[:, 2]
    grad_gate = (gout_t * mix_out).astype(BF16)
    grad_key = (grad_signal * conv_val).astype(BF16)
    grad_conv = grad_signal * key_t
    value_sum = taps[0] * grad_conv
    for tap_index in range(1, tap_count):
        value_sum = value_sum + taps[tap_index] * shift_ahead(grad_conv, tap_index, lane)
    grad_value = value_sum.astype(BF16)
    tap_rows = [jnp.sum(grad_conv * value_shifted[j], axis=(0, 2)) for j in range(tap_count)]
    grad_taps = lax.all_gather(jnp.stack(tap_rows, axis=0), "seq", axis=1, tiled=True)

    outs = jnp.stack([grad_gate, grad_key, grad_value])
    outs = from_tokens_in_lanes(lax.all_to_all(outs, "seq", split_axis=1, concat_axis=1, tiled=True))
    grad_filter = from_tokens_in_lanes(
        lax.all_to_all(grad_filter, "seq", split_axis=0, concat_axis=0, tiled=True)
    )

    swap = [(a * n_chan + b, b * n_chan + a) for a in range(n_seq) for b in range(n_chan)]
    value_swapped = lax.ppermute(grad_value, ("seq", "chan"), swap)
    value_cols = lax.all_gather(value_swapped, "chan", axis=0, tiled=False)
    blocks, width = value_t.shape[0], value_t.shape[2]
    inputs_3 = inputs_all.reshape(blocks, width, inputs_all.shape[1])
    grad_proj = jnp.einsum("pmi,cpom->ico", inputs_3, value_cols, preferred_element_type=F32)
    grad_proj = grad_proj.reshape(grad_proj.shape[0], -1)
    return (outs[0], outs[1], outs[2], grad_taps, grad_filter, grad_proj)


def solution(mesh):
    assert mesh.shape["seq"] == mesh.shape["chan"]
    in_specs = (
        P("seq", "chan"),
        P("seq", "chan"),
        P("seq", "chan"),
        P("seq", "chan"),
        P(None, "chan"),
        P("seq", "chan"),
        P("seq", "chan"),
    )
    out_specs = (
        P("seq", "chan"),
        P("seq", "chan"),
        P("seq", "chan"),
        P(None, "chan"),
        P("seq", "chan"),
        P("chan", "seq"),
    )
    return jax.shard_map(
        on_device, mesh=mesh, in_specs=in_specs, out_specs=out_specs, check_vma=False
    )
```

profile of v0, /device:TPU:224, one launch (start us, length us, event | category | flops | bytes accessed | tf_op | source)
XLA Modules:
  0.0 155.4 jit_solution(6143365006026483340)
XLA Ops:
  7.2 1.8 %copy.113 = f32[128,512]{0,1:T(8,128)} copy(f32[128,512]{1,0:T(8,128)} %param.18) | data formatting | bytes 524288 | tf_op args[5]
  9.0 7.0 %all-to-all-start.1 = ((f32[16,32,128]{2,1,0:T(8,128)}), f32[16,32,128]{2,1,0:T(8,128)S(1)}, u32[]{:S(2)}, u32[]{:S(2)}) async-start(f32[16,32,128]{2,1,0:T(8,128)} %bitcast.11), calls=%async_computation.1 | async-start | bytes 524288 | tf_op jit(solution)/shard_map/all_to_all | solution.py:115
  16.1 0.7 all-gather.5.cloned.1.call-update
  16.8 1.0 copy.107
  17.8 1.0 copy.108
  19.2 0.8 copy.111
  20.1 4.7 %all-to-all-done.1 = f32[16,32,128]{2,1,0:T(8,128)S(1)} async-done(((f32[16,32,128]{2,1,0:T(8,128)}), f32[16,32,128]{2,1,0:T(8,128)S(1)}, u32[]{:S(2)}, u32[]{:S(2)}) %all-to-all-start.1) | async-done | bytes 262176 | tf_op jit(solution)/shard_map/all_to_all | solution.py:115
  24.8 3.6 %all-to-all-start = ((bf16[4,16,32,128]{3,2,0,1:T(8,128)(2,1)}), bf16[4,16,32,128]{3,2,0,1:T(8,128)(2,1)S(1)}, u32[]{:S(2)}, u32[]{:S(2)}) async-start(bf16[4,16,32,128]{3,2,0,1:T(8,128)(2,1)} %copy.111), calls=%async_computation | async-start | bytes 1048576 | tf_op jit(solution)/shard_map/all_to_all | solution.py:114
  28.4 0.6 iota_compare_fusion.2
  29.0 0.6 iota_compare_fusion
  29.7 0.6 slice_bitcast_fusion.8
  30.2 0.9 copy.183
  31.1 7.7 %all-to-all-done = bf16[4,16,32,128]{3,2,0,1:T(8,128)(2,1)S(1)} async-done(((bf16[4,16,32,128]{3,2,0,1:T(8,128)(2,1)}), bf16[4,16,32,128]{3,2,0,1:T(8,128)(2,1)S(1)}, u32[]{:S(2)}, u32[]{:S(2)}) %all-to-all-start) | async-done | bytes 524320 | tf_op jit(solution)/shard_map/all_to_all | solution.py:114
  38.8 0.7 fusion.59
  39.6 1.2 slice_bitcast_fusion.14
  40.7 1.1 slice_bitcast_fusion.12
  41.8 1.0 slice_bitcast_fusion.16
  43.3 0.2 copy.118
  43.5 0.8 copy.119
  44.3 0.9 copy.120
  45.2 1.0 fusion.18
  46.2 1.1 fusion.20
  47.4 2.7 %fusion.12 = f32[64,3,32,128]{3,0,2,1:T(8,128)S(1)} fusion(f32[64,16,1,1]{0,1,3,2:T(8,128)S(1)} %copy-done.29, f32[16,1,32,128]{3,0,2,1:T(8,128)S(1)} %fusion.18, f32[16,1,32,128]{3,0,2,1:T(8,128)S(1)} %fusion.20, f32[16,1,32,128]{3,0,2,1:T(8,128)S(1)} %bitcast.157), kind=kOutput, calls=%fused_computation.20 | convolution fusion | flops 151388160 | bytes 3936256 | tf_op jit(solution)/shard_map/kp,pscm->kscm/dot_general | solution.py:45
  50.1 0.5 multiply_subtract_fusion.1
  50.6 0.3 copy-done.15
  51.0 3.3 %fusion.10 = f32[32,3,32,256]{3,2,1,0:T(8,128)S(1)} fusion(f32[128,256,1,1]{1,0,3,2:T(8,128)S(1)} %copy-done.15, f32[32,3,32,128]{3,0,2,1:T(8,128)S(1)} %get-tuple-element.37), kind=kOutput, calls=%fused_computation.14 | convolution fusion | flops 1207959552 | bytes 4849664 | tf_op jit(solution)/shard_map/kscm,mn->kscn/dot_general | solution.py:49
  54.3 3.3 %convolution_add_fusion.1 = f32[32,3,32,256]{3,2,1,0:T(8,128)S(1)} fusion(f32[32,3,32,256]{3,2,1,0:T(8,128)S(1)} %fusion.10, f32[128,256,1,1]{1,0,3,2:T(8,128)S(1)} %copy-done.13, f32[32,3,32,128]{3,0,2,1:T(8,128)S(1)} %get-tuple-element.36), kind=kOutput, calls=%fused_computation.7 | convolution fusion | flops 1208745984 | bytes 7995392 | tf_op jit(solution)/shard_map/kscm,mn->kscn/dot_general | solution.py:49
  57.7 0.2 multiply_subtract_fusion.3
  57.9 0.5 multiply_add_fusion.2
  58.7 0.7 copy-done.14
  59.5 3.2 %fusion.7 = f32[32,3,32,256]{3,0,2,1:T(8,128)S(1)} fusion(f32[128,256,1,1]{1,0,3,2:T(8,128)S(1)} %copy-done.14, f32[32,3,32,128]{3,2,1,0:T(8,128)S(1)} %pad_maximum_fusion), kind=kOutput, calls=%fused_computation.11 | convolution fusion | flops 1207959552 | bytes 4849664 | tf_op jit(solution)/shard_map/kscn,nm->kscm/dot_general | solution.py:71
  62.7 3.2 %convolution_add_fusion = f32[32,3,32,256]{3,0,2,1:T(8,128)S(1)} fusion(f32[32,3,32,256]{3,0,2,1:T(8,128)S(1)} %fusion.7, f32[128,256,1,1]{1,0,3,2:T(8,128)S(1)} %copy-done.12, f32[32,3,32,128]{3,2,1,0:T(8,128)S(1)} %pad_maximum_fusion.1), kind=kOutput, calls=%fused_computation.6 | convolution fusion | flops 1208745984 | bytes 7995392 | tf_op jit(solution)/shard_map/kscn,nm->kscm/dot_general | solution.py:71
  65.9 0.5 multiply_subtract_fusion
  66.3 0.2 copy-done.28
  66.6 1.6 %fusion = f32[16,3,32,128]{3,0,2,1:T(8,128)S(1)} fusion(f32[16,64,1,1]{1,0,3,2:T(8,128)S(1)} %copy-done.28, f32[32,3,32,128]{3,0,2,1:T(8,128)S(1)} %get-tuple-element.35, f32[32,3,32,128]{3,0,2,1:T(8,128)S(1)} %get-tuple-element.34), kind=kOutput, calls=%fused_computation | convolution fusion | flops 151781376 | bytes 3936256 | tf_op jit(solution)/shard_map/pk,kscm->pscm/dot_general | solution.py:78
  68.2 1.7 %multiply_reduce_fusion = (f32[32]{0:T(128)}, f32[32]{0:T(128)}, f32[32]{0:T(128)}, f32[16,32,128]{2,0,1:T(8,128)S(1)}) fusion(bf16[1,16,32,128]{3,2,0,1:T(8,128)(2,1)S(1)} %get-tuple-element.47, f32[16,32,126]{2,0,1:T(8,128)S(1)} %copy-done.7, f32[16,32,2]{2,0,1:T(8,128)S(1)} %get-tuple-element.67, f32[16,32,126]{2,0,1:T(8,128)S(1)} %copy-done.8, ...), kind=kLoop, calls=%fused_computation.83 | loop fusion | flops 982944 | bytes 1835648 | tf_op jit(solution)/shard_map/reduce_sum | solution.py:138
  70.0 0.2 pad_slice_fusion.1
  70.2 0.2 pad_slice_fusion.3
  70.8 0.3 copy-done.22
  71.1 0.5 fusion.45
  71.6 2.1 %collective-permute-start = (bf16[16,32,128]{2,0,1:T(8,128)(2,1)S(1)}, bf16[16,32,128]{2,0,1:T(8,128)(2,1)S(1)}, u32[]{:S(2)}, u32[]{:S(2)}) collective-permute-start(bf16[16,32,128]{2,0,1:T(8,128)(2,1)S(1)} %fusion.45), channel_id=1, source_target_pairs={{0,0},{1,16},{2,32},{3,48},{4,64},{5,80},{6,96},{7,112},{8,128},{9... | collective-permute-start | bytes 393224 | tf_op jit(solution)/shard_map/ppermute | solution.py:148
  73.8 18.9 %collective-permute-done = bf16[16,32,128]{2,0,1:T(8,128)(2,1)S(1)} collective-permute-done((bf16[16,32,128]{2,0,1:T(8,128)(2,1)S(1)}, bf16[16,32,128]{2,0,1:T(8,128)(2,1)S(1)}, u32[]{:S(2)}, u32[]{:S(2)}) %collective-permute-start) | collective-permute-done | bytes 131104 | tf_op jit(solution)/shard_map/ppermute | solution.py:148
  92.6 0.6 copy-done.18
  93.3 0.8 copy.130
  94.1 0.8 copy.132
  94.8 0.2 copy.127
  95.1 0.2 copy.129
  95.3 0.9 copy.131
  96.2 1.6 %copy.133 = f32[1,16,32,1]{3,1,2,0:T(8,128)} copy(f32[1,16,32,1]{2,1,3,0:T(8,128)} %bitcast.167) | data formatting | bytes 4096 | tf_op jit(solution)/shard_map/jit(_roll_static)/concatenate | solution.py:89
  97.8 0.8 copy.137
  98.6 4.2 %all-to-all-start.3 = ((f32[16,32,128]{2,1,0:T(8,128)}), f32[16,32,128]{2,1,0:T(8,128)}, u32[]{:S(2)}, u32[]{:S(2)}) async-start(f32[16,32,128]{2,1,0:T(8,128)} %copy.137), calls=%async_computation.3 | async-start | bytes 524288 | tf_op jit(solution)/shard_map/all_to_all | solution.py:144
  102.9 1.5 fusion.19
  104.5 0.5 fusion.34
  105.1 0.8 copy.134
  105.9 5.6 %all-to-all-done.3 = f32[16,32,128]{2,1,0:T(8,128)} async-done(((f32[16,32,128]{2,1,0:T(8,128)}), f32[16,32,128]{2,1,0:T(8,128)}, u32[]{:S(2)}, u32[]{:S(2)}) %all-to-all-start.3) | async-done | bytes 262176 | tf_op jit(solution)/shard_map/all_to_all | solution.py:144
  111.5 3.6 %all-to-all-start.2 = ((bf16[3,16,32,128]{3,2,0,1:T(8,128)(2,1)}), bf16[3,16,32,128]{3,2,0,1:T(8,128)(2,1)S(1)}, u32[]{:S(2)}, u32[]{:S(2)}) async-start(bf16[3,16,32,128]{3,2,0,1:T(8,128)(2,1)} %copy.134), calls=%async_computation.2 | async-start | bytes 786432 | tf_op jit(solution)/shard_map/all_to_all | solution.py:142
  115.1 23.8 %all-gather.1 = f32[16,32,3]{1,2,0:T(4,128)S(1)} all-gather(f32[1,32,3]{1,2,0:T(4,128)S(1)} %maximum_bitcast_fusion), channel_id=1, replica_groups=mesh['seq'=16,'chan'=16] {'seq'}, dimensions={0}, use_global_device_ids=true | all-gather | bytes 6528 | tf_op jit(solution)/shard_map/all_gather | solution.py:139
  138.8 0.7 reshape.464
  139.5 1.8 %copy.142 = f32[128,512]{1,0:T(8,128)} copy(f32[128,512]{0,1:T(8,128)} %bitcast.71) | data formatting | bytes 524288
  141.4 0.8 copy.139
  142.2 0.8 copy.140
  142.9 0.8 copy.141
  143.7 3.6 %fusion.4 = f32[16,32,512,1]{2,1,3,0:T(8,128)S(1)} fusion(bf16[16,128,512,1]{2,1,0,3:T(8,128)(2,1)} %bitcast.172, bf16[16,16,32,128]{3,1,0,2:T(8,128)(2,1)} %bitcast.173), kind=kOutput, calls=%fused_computation.4 | convolution fusion | flops 1073741824 | bytes 5242880 | tf_op jit(solution)/shard_map/pmi,cpom->ico/dot_general | solution.py:152
  147.3 1.3 copy.143
  (102 shorter events, 2.0 us)
Async XLA Ops:
  7.2 22.4 %copy-start = (f32[3,512]{1,0:T(4,128)S(1)}, f32[3,512]{1,0:T(4,128)}, u32[]{:S(2)}) copy-start(f32[3,512]{1,0:T(4,128)} %param.17) | copy-start | bytes 18436
  7.2 11.7 %copy-start.16 = (bf16[128,512]{1,0:T(8,128)(2,1)S(1)}, bf16[128,512]{1,0:T(8,128)(2,1)}, u32[]{:S(2)}) copy-start(bf16[128,512]{1,0:T(8,128)(2,1)} %param.16) | copy-start | bytes 393220
  7.2 11.8 %copy-start.17 = (bf16[128,512]{1,0:T(8,128)(2,1)S(1)}, bf16[128,512]{1,0:T(8,128)(2,1)}, u32[]{:S(2)}) copy-start(bf16[128,512]{1,0:T(8,128)(2,1)} %param.19) | copy-start | bytes 393220
  9.0 15.7 %all-to-all-start.1 = ((f32[16,32,128]{2,1,0:T(8,128)}), f32[16,32,128]{2,1,0:T(8,128)S(1)}, u32[]{:S(2)}, u32[]{:S(2)}) async-start(f32[16,32,128]{2,1,0:T(8,128)} %bitcast.11), calls=%async_computation.1 | async-start | bytes 524288 | tf_op jit(solution)/shard_map/all_to_all | solution.py:115
  16.1 127.6 %all-gather.5.cloned.1.call-start = ((), (), s32[]{:S(2)}) async-start(), calls=%async_computation.4 | async-start | bytes 2228224 | tf_op jit(solution)/shard_map/all_gather | solution.py:111
  24.8 14.0 %all-to-all-start = ((bf16[4,16,32,128]{3,2,0,1:T(8,128)(2,1)}), bf16[4,16,32,128]{3,2,0,1:T(8,128)(2,1)S(1)}, u32[]{:S(2)}, u32[]{:S(2)}) async-start(bf16[4,16,32,128]{3,2,0,1:T(8,128)(2,1)} %copy.111), calls=%async_computation | async-start | bytes 1048576 | tf_op jit(solution)/shard_map/all_to_all | solution.py:114
  28.3 115.3 %all-gather.7.cloned.1.call-start = ((), (), s32[]{:S(2)}) async-start(), calls=%async_computation.5 | async-start | bytes 2228224 | tf_op jit(solution)/shard_map/all_gather | solution.py:149
  45.2 2.2 %copy-start.11 = (f32[16,32,128]{2,0,1:T(8,128)S(1)}, f32[16,32,128]{2,0,1:T(8,128)}, u32[]{:S(2)}) copy-start(f32[16,32,128]{2,0,1:T(8,128)} %copy.183) | copy-start | bytes 786436
  45.2 2.2 %copy-start.29 = (f32[64,16,1,1]{0,1,3,2:T(8,128)S(1)}, f32[64,16,1,1]{0,1,3,2:T(8,128)}, u32[]{:S(2)}) copy-start(f32[64,16,1,1]{0,1,3,2:T(8,128)} %constant.51) | copy-start | bytes 12292
  47.4 2.7 %copy-start.20 = (f32[32,128]{1,0:T(8,128)S(1)}, f32[32,128]{1,0:T(8,128)}, u32[]{:S(2)}) copy-start(f32[32,128]{1,0:T(8,128)} %constant.44) | copy-start | bytes 49156
  47.4 2.7 %copy-start.21 = (f32[32,128]{1,0:T(8,128)S(1)}, f32[32,128]{1,0:T(8,128)}, u32[]{:S(2)}) copy-start(f32[32,128]{1,0:T(8,128)} %constant.45) | copy-start | bytes 49156
  50.1 0.9 copy-start.15
  51.0 3.3 %copy-start.13 = (f32[128,256,1,1]{1,0,3,2:T(8,128)S(1)}, f32[128,256,1,1]{1,0,3,2:T(8,128)}, u32[]{:S(2)}) copy-start(f32[128,256,1,1]{1,0,3,2:T(8,128)} %constant.53) | copy-start | bytes 393220
  58.5 0.9 copy-start.14
  59.5 3.2 %copy-start.12 = (f32[128,256,1,1]{1,0,3,2:T(8,128)S(1)}, f32[128,256,1,1]{1,0,3,2:T(8,128)}, u32[]{:S(2)}) copy-start(f32[128,256,1,1]{1,0,3,2:T(8,128)} %constant.55) | copy-start | bytes 393220
  65.8 0.7 copy-start.28
  66.5 1.6 %copy-start.7 = (f32[16,32,126]{2,0,1:T(8,128)S(1)}, f32[16,32,126]{2,0,1:T(8,128)}, u32[]{:S(2)}) copy-start(f32[16,32,126]{2,0,1:T(8,128)} %get-tuple-element.70) | copy-start | bytes 774148
  66.5 1.6 %copy-start.8 = (f32[16,32,126]{2,0,1:T(8,128)S(1)}, f32[16,32,126]{2,0,1:T(8,128)}, u32[]{:S(2)}) copy-start(f32[16,32,126]{2,0,1:T(8,128)} %get-tuple-element.90) | copy-start | bytes 774148
  66.5 1.6 %copy-start.9 = (f32[16,32,127]{2,0,1:T(8,128)S(1)}, f32[16,32,127]{2,0,1:T(8,128)}, u32[]{:S(2)}) copy-start(f32[16,32,127]{2,0,1:T(8,128)} %get-tuple-element.79) | copy-start | bytes 780292
  66.5 1.6 %copy-start.10 = (f32[16,32,127]{2,0,1:T(8,128)S(1)}, f32[16,32,127]{2,0,1:T(8,128)}, u32[]{:S(2)}) copy-start(f32[16,32,127]{2,0,1:T(8,128)} %get-tuple-element.96) | copy-start | bytes 780292
  66.6 1.7 %copy-start.30 = (pred[128]{0:T(512)(128)(4,1)S(1)}, pred[128]{0:T(512)(128)(4,1)}, u32[]{:S(2)}) copy-start(pred[128]{0:T(512)(128)(4,1)} %get-tuple-element.88) | copy-start | bytes 388
  66.6 1.7 %copy-start.32 = (pred[128]{0:T(512)(128)(4,1)S(1)}, pred[128]{0:T(512)(128)(4,1)}, u32[]{:S(2)}) copy-start(pred[128]{0:T(512)(128)(4,1)} %get-tuple-element.89) | copy-start | bytes 388
  70.4 0.7 copy-start.22
  70.4 0.7 copy-start.24
  70.4 0.7 copy-start.26
  70.4 0.7 copy-start.34
  70.4 0.7 copy-start.35
  71.1 23.9 %copy-start.19 = (f32[16,32,1]{1,0,2:T(8,128)S(1)}, f32[16,32,1]{1,0,2:T(8,128)}, u32[]{:S(2)}) copy-start(f32[16,32,1]{1,0,2:T(8,128)} %copy.119) | copy-start | bytes 6148
  71.6 21.0 %collective-permute-start = (bf16[16,32,128]{2,0,1:T(8,128)(2,1)S(1)}, bf16[16,32,128]{2,0,1:T(8,128)(2,1)S(1)}, u32[]{:S(2)}, u32[]{:S(2)}) collective-permute-start(bf16[16,32,128]{2,0,1:T(8,128)(2,1)S(1)} %fusion.45), channel_id=1, source_target_pairs={{0,0},{1,16},{2,32},{3,48},{4,64},{5,80},{6,96},{7,112},{8,128},{9... | collective-permute-start | bytes 393224 | tf_op jit(solution)/shard_map/ppermute | solution.py:148
  92.6 0.7 copy-start.18
  98.6 12.9 %all-to-all-start.3 = ((f32[16,32,128]{2,1,0:T(8,128)}), f32[16,32,128]{2,1,0:T(8,128)}, u32[]{:S(2)}, u32[]{:S(2)}) async-start(f32[16,32,128]{2,1,0:T(8,128)} %copy.137), calls=%async_computation.3 | async-start | bytes 524288 | tf_op jit(solution)/shard_map/all_to_all | solution.py:144
  102.8 1.6 %copy-start.1 = (f32[1,16,32,2]{3,1,2,0:T(8,128)S(1)}, f32[1,16,32,2]{3,1,2,0:T(8,128)}, u32[]{:S(2)}) copy-start(f32[1,16,32,2]{3,1,2,0:T(8,128)} %get-tuple-element.65) | copy-start | bytes 12292
  102.8 1.6 %copy-start.2 = (f32[1,16,32,2]{3,1,2,0:T(8,128)S(1)}, f32[1,16,32,2]{3,1,2,0:T(8,128)}, u32[]{:S(2)}) copy-start(f32[1,16,32,2]{3,1,2,0:T(8,128)} %get-tuple-element.95) | copy-start | bytes 12292
  102.8 1.6 %copy-start.3 = (f32[1,16,32,126]{3,1,2,0:T(8,128)S(1)}, f32[1,16,32,126]{3,1,2,0:T(8,128)}, u32[]{:S(2)}) copy-start(f32[1,16,32,126]{3,1,2,0:T(8,128)} %get-tuple-element.68) | copy-start | bytes 774148
  102.8 1.6 %copy-start.4 = (f32[1,16,32,126]{3,1,2,0:T(8,128)S(1)}, f32[1,16,32,126]{3,1,2,0:T(8,128)}, u32[]{:S(2)}) copy-start(f32[1,16,32,126]{3,1,2,0:T(8,128)} %get-tuple-element.92) | copy-start | bytes 774148
  102.8 1.6 %copy-start.5 = (f32[1,16,32,127]{3,1,2,0:T(8,128)S(1)}, f32[1,16,32,127]{3,1,2,0:T(8,128)}, u32[]{:S(2)}) copy-start(f32[1,16,32,127]{3,1,2,0:T(8,128)} %get-tuple-element.77) | copy-start | bytes 780292
  102.8 1.6 %copy-start.6 = (f32[1,16,32,127]{3,1,2,0:T(8,128)S(1)}, f32[1,16,32,127]{3,1,2,0:T(8,128)}, u32[]{:S(2)}) copy-start(f32[1,16,32,127]{3,1,2,0:T(8,128)} %get-tuple-element.98) | copy-start | bytes 780292
  102.8 1.6 %copy-start.23 = (f32[32]{0:T(128)S(1)}, f32[32]{0:T(128)}, u32[]{:S(2)}) copy-start(f32[32]{0:T(128)} %get-tuple-element.85) | copy-start | bytes 388
  102.8 1.6 %copy-start.25 = (f32[32]{0:T(128)S(1)}, f32[32]{0:T(128)}, u32[]{:S(2)}) copy-start(f32[32]{0:T(128)} %get-tuple-element.86) | copy-start | bytes 388
  102.8 1.6 %copy-start.27 = (f32[32]{0:T(128)S(1)}, f32[32]{0:T(128)}, u32[]{:S(2)}) copy-start(f32[32]{0:T(128)} %get-tuple-element.87) | copy-start | bytes 388
  102.9 1.6 %copy-start.31 = (pred[128]{0:T(512)(128)(4,1)S(1)}, pred[128]{0:T(512)(128)(4,1)}, u32[]{:S(2)}) copy-start(pred[128]{0:T(512)(128)(4,1)} %get-tuple-element.88) | copy-start | bytes 388
  102.9 1.6 %copy-start.33 = (pred[128]{0:T(512)(128)(4,1)S(1)}, pred[128]{0:T(512)(128)(4,1)}, u32[]{:S(2)}) copy-start(pred[128]{0:T(512)(128)(4,1)} %get-tuple-element.89) | copy-start | bytes 388
  105.0 10.1 %copy-start.36 = (f32[32]{0:T(128)S(1)}, f32[32]{0:T(128)}, u32[]{:S(2)}) copy-start(f32[32]{0:T(128)} %get-tuple-element.30) | copy-start | bytes 388
  105.0 10.1 %copy-start.37 = (f32[32]{0:T(128)S(1)}, f32[32]{0:T(128)}, u32[]{:S(2)}) copy-start(f32[32]{0:T(128)} %get-tuple-element.31) | copy-start | bytes 388
  105.0 10.1 %copy-start.38 = (f32[32]{0:T(128)S(1)}, f32[32]{0:T(128)}, u32[]{:S(2)}) copy-start(f32[32]{0:T(128)} %get-tuple-element.32) | copy-start | bytes 388
  111.5 29.9 %all-to-all-start.2 = ((bf16[3,16,32,128]{3,2,0,1:T(8,128)(2,1)}), bf16[3,16,32,128]{3,2,0,1:T(8,128)(2,1)S(1)}, u32[]{:S(2)}, u32[]{:S(2)}) async-start(bf16[3,16,32,128]{3,2,0,1:T(8,128)(2,1)} %copy.134), calls=%async_computation.2 | async-start | bytes 786432 | tf_op jit(solution)/shard_map/all_to_all | solution.py:142
Sparse Core Ops, SparseCore 0:
  19.3 50.4 all-gather.4
  93.4 35.0 all-gather.6
where the time goes:
time: 156 us; the launch traced here: 155 us
  waiting for transfers between devices  37.5 us (24%)
  local copies, waits for them, and re-layouts  28.2 us (18%)
  blocking collectives  23.8 us (15%)
  matrix products  20.8 us (13%)
  starting transfers between devices  20.6 us (13%)
  between operations  14.9 us (10%)
  other arithmetic  9.71 us (6%)
    all_gather x1, blocking collectives, on_device(): lax.all_gather(jnp.stack(tap_rows, axis=0), 'seq', axis=1, tiled=True)  23.8 us
    ppermute x1, waiting for transfers between devices, on_device(): value_swapped = lax.ppermute(grad_value, ('seq', 'chan'), swap)  18.9 us
    unnamed x89, local copies, waits for them, and re-layouts  12.6 us
    all_to_all x1, waiting for transfers between devices, on_device(): lax.all_to_all(halves, 'seq', split_axis=1, concat_axis=1, tiled=True)  7.69 us
    all_to_all x1, starting transfers between devices, on_device(): lax.all_to_all(to_tokens_in_lanes(long_filter, n_seq), 'seq', split_axis=...  7.03 us
    all_to_all x1, waiting for transfers between devices, on_device(): lax.all_to_all(grad_filter, 'seq', split_axis=0, concat_axis=0, tiled=True)  5.55 us
    all_to_all x1, waiting for transfers between devices, on_device(): lax.all_to_all(to_tokens_in_lanes(long_filter, n_seq), 'seq', split_axis=...  4.7 us
    concatenate x5, local copies, waits for them, and re-layouts, shift_back(): jnp.roll(x, by, axis=-1)  4.32 us
  transfers between devices with their start and end apart: 7, of which 4 were waited for; matrix products, arithmetic and copies ran while one was open for 32% of the time, Pallas kernels for 0%

commit v1 on v0

--- a/solution.py
+++ b/solution.py
@@ -101,6 +101,15 @@
     return jnp.swapaxes(block.reshape(lead + (parts * sub, rows)), -1, -2)
 
 
+def split_words(x):
+    rounded = lax.reduce_precision(x, exponent_bits=8, mantissa_bits=7)
+    return rounded.astype(BF16), (x - rounded).astype(BF16)
+
+
+def join_words(high, low):
+    return high.astype(F32) + low.astype(F32)
+
+
 def on_device(layer_input, value_pre, gate_act, key_act, short_taps, long_filter, grad_out):
     n_seq = lax.axis_size("seq")
     n_chan = lax.axis_size("chan")
@@ -110,13 +119,14 @@
 
     inputs_all = lax.all_gather(layer_input, "seq", axis=0, tiled=True)
 
-    halves = to_tokens_in_lanes(jnp.stack([value_pre, gate_act, key_act, grad_out]), n_seq)
-    halves = lax.all_to_all(halves, "seq", split_axis=1, concat_axis=1, tiled=True)
-    filt = lax.all_to_all(to_tokens_in_lanes(long_filter, n_seq), "seq", split_axis=0, concat_axis=0, tiled=True)
-    value_t = halves[0].astype(F32)
-    gate_t = halves[1].astype(F32)
-    key_t = halves[2].astype(F32)
-    gout_t = halves[3].astype(F32)
+    filt_high, filt_low = split_words(long_filter)
+    sent = to_tokens_in_lanes(jnp.stack([value_pre, gate_act, key_act, grad_out, filt_high, filt_low]), n_seq)
+    got = lax.all_to_all(sent, "seq", split_axis=1, concat_axis=1, tiled=True)
+    value_t = got[0].astype(F32)
+    gate_t = got[1].astype(F32)
+    key_t = got[2].astype(F32)
+    gout_t = got[3].astype(F32)
+    filt = join_words(got[4], got[5])
     taps = lax.dynamic_slice_in_dim(short_taps, me * sub, sub, axis=1)[:, :, None]
     lane = lax.broadcasted_iota(jnp.int32, value_t.shape, 2)
 
@@ -135,19 +145,29 @@
     for tap_index in range(1, tap_count):
         value_sum = value_sum + taps[tap_index] * shift_ahead(grad_conv, tap_index, lane)
     grad_value = value_sum.astype(BF16)
-    tap_rows = [jnp.sum(grad_conv * value_shifted[j], axis=(0, 2)) for j in range(tap_count)]
-    grad_taps = lax.all_gather(jnp.stack(tap_rows, axis=0), "seq", axis=1, tiled=True)
-
-    outs = jnp.stack([grad_gate, grad_key, grad_value])
-    outs = from_tokens_in_lanes(lax.all_to_all(outs, "seq", split_axis=1, concat_axis=1, tiled=True))
-    grad_filter = from_tokens_in_lanes(
-        lax.all_to_all(grad_filter, "seq", split_axis=0, concat_axis=0, tiled=True)
-    )
 
     swap = [(a * n_chan + b, b * n_chan + a) for a in range(n_seq) for b in range(n_chan)]
     value_swapped = lax.ppermute(grad_value, ("seq", "chan"), swap)
-    value_cols = lax.all_gather(value_swapped, "chan", axis=0, tiled=False)
-    blocks, width = value_t.shape[0], value_t.shape[2]
+    value_cols = lax.all_to_all(
+        jnp.broadcast_to(value_swapped[None], (n_chan,) + value_swapped.shape),
+        "chan", split_axis=0, concat_axis=0, tiled=True,
+    )
+
+    tap_rows = jnp.stack([jnp.sum(grad_conv * value_shifted[j], axis=(0, 2)) for j in range(tap_count)])
+    taps_high, taps_low = split_words(tap_rows)
+    width = value_t.shape[2]
+    taps_slab = jnp.pad(jnp.concatenate([taps_high, taps_low], axis=0).T, ((0, 0), (0, width - 2 * tap_count)))
+    taps_slab = jnp.broadcast_to(taps_slab[None], value_t.shape)
+    gf_high, gf_low = split_words(grad_filter)
+    outs = jnp.stack([grad_gate, grad_key, grad_value, gf_high, gf_low, taps_slab])
+    outs = lax.all_to_all(outs, "seq", split_axis=1, concat_axis=1, tiled=True)
+    taps_got = outs[5, :, :, : 2 * tap_count]
+    grad_taps = join_words(taps_got[..., :tap_count], taps_got[..., tap_count:])
+    grad_taps = jnp.transpose(grad_taps, (2, 0, 1)).reshape(tap_count, -1)
+    outs = from_tokens_in_lanes(outs[:5])
+    grad_filter = join_words(outs[3], outs[4])
+
+    blocks = value_t.shape[0]
     inputs_3 = inputs_all.reshape(blocks, width, inputs_all.shape[1])
     grad_proj = jnp.einsum("pmi,cpom->ico", inputs_3, value_cols, preferred_element_type=F32)
     grad_proj = grad_proj.reshape(grad_proj.shape[0], -1)

time: 156 us -> 180 us (1.15)
  the two profiles are of different devices: /device:TPU:224 before, /device:TPU:1 now
where the time goes in v1:
time: 180 us; the launch traced here: 179 us
  waiting for transfers between devices  72.6 us (40%)
  local copies, waits for them, and re-layouts  32.6 us (18%)
  starting transfers between devices  28.3 us (16%)
  matrix products  20.7 us (12%)
  between operations  14.8 us (8%)
  other arithmetic  10.4 us (6%)
    all_to_all x1, waiting for transfers between devices, on_device(): lax.all_to_all(jnp.broadcast_to(value_swapped[None], (n_chan,) + value_sw...  26.1 us
    all_gather x1, waiting for transfers between devices, on_device(): inputs_all = lax.all_gather(layer_input, 'seq', axis=0, tiled=True)  18.9 us
    ppermute x1, waiting for transfers between devices, on_device(): value_swapped = lax.ppermute(grad_value, ('seq', 'chan'), swap)  16.2 us
    all_to_all x1, starting transfers between devices, on_device(): lax.all_to_all(jnp.broadcast_to(value_swapped[None], (n_chan,) + value_sw...  11.4 us
    all_to_all x1, waiting for transfers between devices, on_device(): got = lax.all_to_all(sent, 'seq', split_axis=1, concat_axis=1, tiled=True)  11.4 us
    unnamed x88, local copies, waits for them, and re-layouts  11.2 us
    all_to_all x1, starting transfers between devices, on_device(): got = lax.all_to_all(sent, 'seq', split_axis=1, concat_axis=1, tiled=True)  7.57 us
    ppermute x1, starting transfers between devices, on_device(): value_swapped = lax.ppermute(grad_value, ('seq', 'chan'), swap)  5.47 us
  transfers between devices with their start and end apart: 5, of which 4 were waited for; matrix products, arithmetic and copies ran while one was open for 5% of the time, Pallas kernels for 0%

profile of v1, /device:TPU:1, one launch (start us, length us, event | category | flops | bytes accessed | tf_op | source)
XLA Modules:
  0.0 179.5 jit_solution(7167104619769685218)
XLA Ops:
  7.2 1.1 copy.112
  8.3 1.0 copy.108
  9.4 1.0 copy.109
  10.4 1.0 copy.110
  11.7 1.0 copy.114
  12.7 7.6 %all-to-all-start = ((bf16[6,16,32,128]{3,2,0,1:T(8,128)(2,1)}), bf16[6,16,32,128]{3,2,0,1:T(8,128)(2,1)S(1)}, u32[]{:S(2)}, u32[]{:S(2)}) async-start(bf16[6,16,32,128]{3,2,0,1:T(8,128)(2,1)} %copy.114), calls=%async_computation | async-start | bytes 1572864 | tf_op jit(solution)/shard_map/all_to_all | solution.py:124
  20.3 0.6 iota_compare_fusion.2
  20.9 0.6 iota_compare_fusion
  21.5 0.6 slice_bitcast_fusion.9
  22.1 11.4 %all-to-all-done = bf16[6,16,32,128]{3,2,0,1:T(8,128)(2,1)S(1)} async-done(((bf16[6,16,32,128]{3,2,0,1:T(8,128)(2,1)}), bf16[6,16,32,128]{3,2,0,1:T(8,128)(2,1)S(1)}, u32[]{:S(2)}, u32[]{:S(2)}) %all-to-all-start) | async-done | bytes 786464 | tf_op jit(solution)/shard_map/all_to_all | solution.py:124
  33.5 0.8 fusion.69
  34.3 1.1 pad_slice_fusion.5
  35.5 1.0 pad_slice_fusion.4
  36.5 1.0 pad_slice_fusion.6
  37.8 0.2 copy.120
  38.0 0.2 copy.121
  38.2 0.8 copy.122
  39.0 0.9 copy.123
  39.9 1.2 fusion.16
  41.1 1.1 fusion.20
  42.3 2.7 %fusion.10 = f32[64,3,32,128]{3,0,2,1:T(8,128)S(1)} fusion(f32[64,16,1,1]{0,1,3,2:T(8,128)S(1)} %copy-done.29, f32[16,1,32,128]{3,0,2,1:T(8,128)S(1)} %get-tuple-element.90, f32[16,1,32,128]{3,0,2,1:T(8,128)S(1)} %fusion.20, f32[16,1,32,128]{3,0,2,1:T(8,128)S(1)} %get-tuple-element.91), kind=kOutput, calls=%fused_computation.18 | convolution fusion | flops 151388160 | bytes 3936256 | tf_op jit(solution)/shard_map/kp,pscm->kscm/dot_general | solution.py:45
  45.0 0.5 multiply_subtract_fusion.1
  45.5 0.3 copy-done.18
  45.9 3.3 %fusion.8 = f32[32,3,32,256]{3,2,1,0:T(8,128)S(1)} fusion(f32[128,256,1,1]{1,0,3,2:T(8,128)S(1)} %copy-done.18, f32[32,3,32,128]{3,0,2,1:T(8,128)S(1)} %get-tuple-element.37), kind=kOutput, calls=%fused_computation.12 | convolution fusion | flops 1207959552 | bytes 4849664 | tf_op jit(solution)/shard_map/kscm,mn->kscn/dot_general | solution.py:49
  49.2 3.3 %convolution_add_fusion.1 = f32[32,3,32,256]{3,2,1,0:T(8,128)S(1)} fusion(f32[32,3,32,256]{3,2,1,0:T(8,128)S(1)} %fusion.8, f32[128,256,1,1]{1,0,3,2:T(8,128)S(1)} %copy-done.16, f32[32,3,32,128]{3,0,2,1:T(8,128)S(1)} %get-tuple-element.36), kind=kOutput, calls=%fused_computation.5 | convolution fusion | flops 1208745984 | bytes 7995392 | tf_op jit(solution)/shard_map/kscm,mn->kscn/dot_general | solution.py:49
  52.6 0.3 multiply_add_fusion.2
  52.9 0.4 multiply_subtract_fusion.3
  53.5 0.7 copy-done.17
  54.2 3.2 %fusion.5 = f32[32,3,32,256]{3,0,2,1:T(8,128)S(1)} fusion(f32[128,256,1,1]{1,0,3,2:T(8,128)S(1)} %copy-done.17, f32[32,3,32,128]{3,2,1,0:T(8,128)S(1)} %pad_maximum_fusion), kind=kOutput, calls=%fused_computation.9 | convolution fusion | flops 1207959552 | bytes 4849664 | tf_op jit(solution)/shard_map/kscn,nm->kscm/dot_general | solution.py:71
  57.6 0.7 copy-done.15
  58.3 3.2 %convolution_add_fusion = f32[32,3,32,256]{3,0,2,1:T(8,128)S(1)} fusion(f32[32,3,32,256]{3,0,2,1:T(8,128)S(1)} %fusion.5, f32[128,256,1,1]{1,0,3,2:T(8,128)S(1)} %copy-done.15, f32[32,3,32,128]{3,2,1,0:T(8,128)S(1)} %pad_maximum_fusion.1), kind=kOutput, calls=%fused_computation.4 | convolution fusion | flops 1208745984 | bytes 7995392 | tf_op jit(solution)/shard_map/kscn,nm->kscm/dot_general | solution.py:71
  61.5 0.5 multiply_subtract_fusion
  62.0 0.2 copy-done.28
  62.2 1.6 fusion
  63.9 1.1 multiply_reduce_fusion
  65.0 0.9 pad_slice_fusion.1
  65.9 0.7 pad_slice_fusion
  66.7 0.9 pad_slice_fusion.3
  67.6 0.9 fusion.70
  68.4 0.8 fusion.71
  69.3 0.9 fusion.72
  70.4 0.2 copy.133
  70.6 0.9 copy.134
  71.7 0.9 copy.136
  72.6 0.9 copy.130
  73.5 1.6 copy.132
  75.1 2.2 %fusion.47 = bf16[6,16,32,128]{3,1,2,0:T(8,128)(2,1)S(1)} fusion(bf16[6,16,32,128]{3,1,2,0:T(8,128)(2,1)S(1)} %fusion.52, f32[1,16,32,126]{3,1,2,0:T(8,128)} %get-tuple-element.92, f32[1,16,32,2]{3,1,2,0:T(8,128)} %get-tuple-element.95, f32[1,16,32,126]{3,1,2,0:T(8,128)} %get-tuple-element.76, f32[1,16,32,2]{3,1,2,0:T(8,128)} %get-tuple-element.73, ...), kind=kLoop, calls=%fused_computation.97 | loop fusion | flops 917504 | bytes 1573504
  77.4 0.7 fusion.48
  78.3 1.1 copy.138
  79.4 3.8 %all-to-all-start.1 = ((bf16[6,16,32,128]{3,2,0,1:T(8,128)(2,1)}), bf16[6,16,32,128]{3,2,0,1:T(8,128)(2,1)S(1)}, u32[]{:S(2)}, u32[]{:S(2)}) async-start(bf16[6,16,32,128]{3,2,0,1:T(8,128)(2,1)} %copy.138), calls=%async_computation.1 | async-start | bytes 1572864 | tf_op jit(solution)/shard_map/all_to_all | solution.py:163
  83.4 0.5 fusion.45
  83.8 5.5 %collective-permute-start = (bf16[16,32,128]{2,0,1:T(8,128)(2,1)S(1)}, bf16[16,32,128]{2,0,1:T(8,128)(2,1)S(1)}, u32[]{:S(2)}, u32[]{:S(2)}) collective-permute-start(bf16[16,32,128]{2,0,1:T(8,128)(2,1)S(1)} %fusion.45), channel_id=1, source_target_pairs={{0,0},{1,16},{2,32},{3,48},{4,64},{5,80},{6,96},{7,112},{8,128},{9... | collective-permute-start | bytes 393224 | tf_op jit(solution)/shard_map/ppermute | solution.py:150
  89.3 16.2 %collective-permute-done = bf16[16,32,128]{2,0,1:T(8,128)(2,1)S(1)} collective-permute-done((bf16[16,32,128]{2,0,1:T(8,128)(2,1)S(1)}, bf16[16,32,128]{2,0,1:T(8,128)(2,1)S(1)}, u32[]{:S(2)}, u32[]{:S(2)}) %collective-permute-start) | collective-permute-done | bytes 131104 | tf_op jit(solution)/shard_map/ppermute | solution.py:150
  105.5 1.8 broadcast_in_dim.2
  107.3 11.4 %all-to-all-start.2 = ((bf16[16,16,32,128]{3,2,1,0:T(8,128)(2,1)}), bf16[16,16,32,128]{3,2,1,0:T(8,128)(2,1)}, u32[]{:S(2)}, u32[]{:S(2)}) async-start(bf16[16,16,32,128]{3,2,1,0:T(8,128)(2,1)} %broadcast_in_dim.2), calls=%async_computation.2 | async-start | bytes 4194304 | tf_op jit(solution)/shard_map/all_to_all | solution.py:151
  118.8 0.8 copy.142
  119.6 0.8 copy.143
  120.4 0.8 copy.144
  121.2 0.8 copy.145
  122.1 0.7 copy.158
  122.8 18.9 %all-gather.2.cloned.1.call-done = bf16[2048,512]{1,0:T(8,128)(2,1)} async-done(((bf16[128,512]{1,0:T(8,128)(2,1)}), bf16[2048,512]{1,0:T(8,128)(2,1)}) %all-gather.2.cloned.1.call-update) | async-done | bytes 2097168 | tf_op jit(solution)/shard_map/all_gather | solution.py:120
  141.7 26.1 %all-to-all-done.2 = bf16[16,16,32,128]{3,2,1,0:T(8,128)(2,1)} async-done(((bf16[16,16,32,128]{3,2,1,0:T(8,128)(2,1)}), bf16[16,16,32,128]{3,2,1,0:T(8,128)(2,1)}, u32[]{:S(2)}, u32[]{:S(2)}) %all-to-all-start.2) | async-done | bytes 2097184 | tf_op jit(solution)/shard_map/all_to_all | solution.py:151
  167.8 3.5 %fusion.76 = f32[16,32,512,1]{2,1,3,0:T(8,128)S(1)} fusion(bf16[16,16,32,128]{3,2,1,0:T(8,128)(2,1)} %all-to-all-done.2, bf16[16,128,512,1]{2,1,0,3:T(8,128)(2,1)} %bitcast.189), kind=kOutput, calls=%fused_computation.156 | convolution fusion | flops 1073741824 | bytes 5242880 | tf_op jit(solution)/shard_map/pmi,cpom->ico/dot_general | solution.py:172
  171.3 1.3 copy.146
  (103 shorter events, 2.0 us)
Async XLA Ops:
  7.2 14.3 %copy-start = (f32[3,512]{1,0:T(4,128)S(1)}, f32[3,512]{1,0:T(4,128)}, u32[]{:S(2)}) copy-start(f32[3,512]{1,0:T(4,128)} %param.17) | copy-start | bytes 18436
  7.2 4.2 %copy-start.19 = (bf16[128,512]{1,0:T(8,128)(2,1)S(1)}, bf16[128,512]{1,0:T(8,128)(2,1)}, u32[]{:S(2)}) copy-start(bf16[128,512]{1,0:T(8,128)(2,1)} %param.19) | copy-start | bytes 393220
  12.7 20.8 %all-to-all-start = ((bf16[6,16,32,128]{3,2,0,1:T(8,128)(2,1)}), bf16[6,16,32,128]{3,2,0,1:T(8,128)(2,1)S(1)}, u32[]{:S(2)}, u32[]{:S(2)}) async-start(bf16[6,16,32,128]{3,2,0,1:T(8,128)(2,1)} %copy.114), calls=%async_computation | async-start | bytes 1572864 | tf_op jit(solution)/shard_map/all_to_all | solution.py:124
  41.1 1.2 copy-start.29
  42.3 2.7 %copy-start.20 = (f32[32,128]{1,0:T(8,128)S(1)}, f32[32,128]{1,0:T(8,128)}, u32[]{:S(2)}) copy-start(f32[32,128]{1,0:T(8,128)} %constant.48) | copy-start | bytes 49156
  42.3 2.7 %copy-start.21 = (f32[32,128]{1,0:T(8,128)S(1)}, f32[32,128]{1,0:T(8,128)}, u32[]{:S(2)}) copy-start(f32[32,128]{1,0:T(8,128)} %constant.49) | copy-start | bytes 49156
  45.0 0.9 copy-start.18
  45.9 3.3 %copy-start.16 = (f32[128,256,1,1]{1,0,3,2:T(8,128)S(1)}, f32[128,256,1,1]{1,0,3,2:T(8,128)}, u32[]{:S(2)}) copy-start(f32[128,256,1,1]{1,0,3,2:T(8,128)} %constant.57) | copy-start | bytes 393220
  53.3 0.9 copy-start.17
  57.4 0.9 copy-start.15
  61.5 0.7 copy-start.28
  62.2 1.6 copy-start.11
  62.2 1.7 copy-start.12
  62.2 1.7 copy-start.13
  62.2 1.7 copy-start.14
  62.2 1.7 copy-start.30
  62.2 1.7 copy-start.31
  72.6 4.7 %copy-start.22 = (f32[32]{0:T(128)S(1)}, f32[32]{0:T(128)}, u32[]{:S(2)}) copy-start(f32[32]{0:T(128)} %get-tuple-element.85) | copy-start | bytes 388
  72.6 4.7 %copy-start.24 = (f32[32]{0:T(128)S(1)}, f32[32]{0:T(128)}, u32[]{:S(2)}) copy-start(f32[32]{0:T(128)} %get-tuple-element.86) | copy-start | bytes 388
  72.6 4.7 %copy-start.26 = (f32[32]{0:T(128)S(1)}, f32[32]{0:T(128)}, u32[]{:S(2)}) copy-start(f32[32]{0:T(128)} %get-tuple-element.87) | copy-start | bytes 388
  72.6 4.7 %copy-start.32 = (pred[128]{0:T(512)(128)(4,1)S(1)}, pred[128]{0:T(512)(128)(4,1)}, u32[]{:S(2)}) copy-start(pred[128]{0:T(512)(128)(4,1)} %get-tuple-element.103) | copy-start | bytes 388
  72.6 4.7 %copy-start.34 = (pred[128]{0:T(512)(128)(4,1)S(1)}, pred[128]{0:T(512)(128)(4,1)}, u32[]{:S(2)}) copy-start(pred[128]{0:T(512)(128)(4,1)} %get-tuple-element.104) | copy-start | bytes 388
  75.1 2.3 %copy-start.3 = (f32[1,16,32,126]{3,1,2,0:T(8,128)S(1)}, f32[1,16,32,126]{3,1,2,0:T(8,128)}, u32[]{:S(2)}) copy-start(f32[1,16,32,126]{3,1,2,0:T(8,128)} %get-tuple-element.58) | copy-start | bytes 774148
  75.1 2.3 %copy-start.4 = (f32[1,16,32,2]{3,1,2,0:T(8,128)S(1)}, f32[1,16,32,2]{3,1,2,0:T(8,128)}, u32[]{:S(2)}) copy-start(f32[1,16,32,2]{3,1,2,0:T(8,128)} %get-tuple-element.60) | copy-start | bytes 12292
  75.1 2.3 %copy-start.5 = (f32[1,16,32,127]{3,1,2,0:T(8,128)S(1)}, f32[1,16,32,127]{3,1,2,0:T(8,128)}, u32[]{:S(2)}) copy-start(f32[1,16,32,127]{3,1,2,0:T(8,128)} %get-tuple-element.64) | copy-start | bytes 780292
  75.1 2.3 %copy-start.6 = (f32[1,16,32,126]{3,1,2,0:T(8,128)S(1)}, f32[1,16,32,126]{3,1,2,0:T(8,128)}, u32[]{:S(2)}) copy-start(f32[1,16,32,126]{3,1,2,0:T(8,128)} %get-tuple-element.54) | copy-start | bytes 774148
  75.1 2.3 %copy-start.7 = (f32[1,16,32,2]{3,1,2,0:T(8,128)S(1)}, f32[1,16,32,2]{3,1,2,0:T(8,128)}, u32[]{:S(2)}) copy-start(f32[1,16,32,2]{3,1,2,0:T(8,128)} %get-tuple-element.56) | copy-start | bytes 12292
  75.1 2.3 %copy-start.8 = (f32[1,16,32,127]{3,1,2,0:T(8,128)S(1)}, f32[1,16,32,127]{3,1,2,0:T(8,128)}, u32[]{:S(2)}) copy-start(f32[1,16,32,127]{3,1,2,0:T(8,128)} %get-tuple-element.62) | copy-start | bytes 780292
  75.1 2.3 %copy-start.9 = (f32[1,16,32,1]{3,1,2,0:T(8,128)S(1)}, f32[1,16,32,1]{3,1,2,0:T(8,128)}, u32[]{:S(2)}) copy-start(f32[1,16,32,1]{3,1,2,0:T(8,128)} %copy.134) | copy-start | bytes 6148
  75.1 2.3 %copy-start.10 = (f32[1,16,32,1]{3,1,2,0:T(8,128)S(1)}, f32[1,16,32,1]{3,1,2,0:T(8,128)}, u32[]{:S(2)}) copy-start(f32[1,16,32,1]{3,1,2,0:T(8,128)} %copy.136) | copy-start | bytes 6148
  78.3 5.0 %copy-start.1 = (f32[16,32,2]{2,0,1:T(8,128)S(1)}, f32[16,32,2]{2,0,1:T(8,128)}, u32[]{:S(2)}) copy-start(f32[16,32,2]{2,0,1:T(8,128)} %get-tuple-element.55) | copy-start | bytes 12292
  78.3 5.0 %copy-start.23 = (f32[32]{0:T(128)S(1)}, f32[32]{0:T(128)}, u32[]{:S(2)}) copy-start(f32[32]{0:T(128)} %get-tuple-element.85) | copy-start | bytes 388
  78.3 5.0 %copy-start.25 = (f32[32]{0:T(128)S(1)}, f32[32]{0:T(128)}, u32[]{:S(2)}) copy-start(f32[32]{0:T(128)} %get-tuple-element.86) | copy-start | bytes 388
  79.4 3.9 %copy-start.2 = (f32[16,32,127]{2,0,1:T(8,128)S(1)}, f32[16,32,127]{2,0,1:T(8,128)}, u32[]{:S(2)}) copy-start(f32[16,32,127]{2,0,1:T(8,128)} %get-tuple-element.61) | copy-start | bytes 780292
  79.4 3.9 %copy-start.27 = (f32[32]{0:T(128)S(1)}, f32[32]{0:T(128)}, u32[]{:S(2)}) copy-start(f32[32]{0:T(128)} %get-tuple-element.87) | copy-start | bytes 388
  79.4 4.0 %copy-start.33 = (pred[128]{0:T(512)(128)(4,1)S(1)}, pred[128]{0:T(512)(128)(4,1)}, u32[]{:S(2)}) copy-start(pred[128]{0:T(512)(128)(4,1)} %get-tuple-element.103) | copy-start | bytes 388
  79.4 4.0 %copy-start.35 = (pred[128]{0:T(512)(128)(4,1)S(1)}, pred[128]{0:T(512)(128)(4,1)}, u32[]{:S(2)}) copy-start(pred[128]{0:T(512)(128)(4,1)} %get-tuple-element.104) | copy-start | bytes 388
  79.4 26.1 %all-to-all-start.1 = ((bf16[6,16,32,128]{3,2,0,1:T(8,128)(2,1)}), bf16[6,16,32,128]{3,2,0,1:T(8,128)(2,1)S(1)}, u32[]{:S(2)}, u32[]{:S(2)}) async-start(bf16[6,16,32,128]{3,2,0,1:T(8,128)(2,1)} %copy.138), calls=%async_computation.1 | async-start | bytes 1572864 | tf_op jit(solution)/shard_map/all_to_all | solution.py:163
  83.2 58.5 %all-gather.2.cloned.1.call-start = ((), (), s32[]{:S(2)}) async-start(), calls=%async_computation.3 | async-start | bytes 2228224 | tf_op jit(solution)/shard_map/all_gather | solution.py:120
  83.8 21.7 %collective-permute-start = (bf16[16,32,128]{2,0,1:T(8,128)(2,1)S(1)}, bf16[16,32,128]{2,0,1:T(8,128)(2,1)S(1)}, u32[]{:S(2)}, u32[]{:S(2)}) collective-permute-start(bf16[16,32,128]{2,0,1:T(8,128)(2,1)S(1)} %fusion.45), channel_id=1, source_target_pairs={{0,0},{1,16},{2,32},{3,48},{4,64},{5,80},{6,96},{7,112},{8,128},{9... | collective-permute-start | bytes 393224 | tf_op jit(solution)/shard_map/ppermute | solution.py:150
  107.3 60.5 %all-to-all-start.2 = ((bf16[16,16,32,128]{3,2,1,0:T(8,128)(2,1)}), bf16[16,16,32,128]{3,2,1,0:T(8,128)(2,1)}, u32[]{:S(2)}, u32[]{:S(2)}) async-start(bf16[16,16,32,128]{3,2,1,0:T(8,128)(2,1)} %broadcast_in_dim.2), calls=%async_computation.2 | async-start | bytes 4194304 | tf_op jit(solution)/shard_map/all_to_all | solution.py:151
Sparse Core Ops, SparseCore 0:
  89.4 52.2 all-gather.1
